TPU v7x, 256 devices: a whole 4x4x8 slice. The times are simulated.
256 devices in a mesh: seq: 64 (over x, z, core), ch: 4 (over y).
Axes of the slice: x: 4, y: 4, z: 8, core: 2. Of those that a mesh axis runs over, the one named last changes fastest.
Arguments:
- inputs: bfloat16 [8192, 4096], P('seq'), may hold values from -6 to 6
- norm_gain: float32 [4096], replicated, may hold values from 0.1 to 1.9
- in_weight: bfloat16 [4096, 3, 1024], P('seq', None, 'ch'), may hold values from -0.09375 to 0.09375
- short_filter: float32 [3, 3, 1024], P(None, None, 'ch'), may hold values from -4 to 4
- long_filter: float32 [8192, 1024], P('seq', 'ch'), may hold values from -2.2 to 2.2
- conv_bias: float32 [1024], P('ch'), may hold values from -4 to 4
- out_weight: bfloat16 [1024, 4096], P('ch', 'seq'), may hold values from -0.1875 to 0.1875
- out_grad: bfloat16 [8192, 4096], P('seq'), may hold values from -6 to 6
Outputs:
- block_out: bfloat16 [8192, 4096], P('seq', 'ch')
- in_grad: bfloat16 [8192, 4096], P('seq')
- filter_grad: float32 [8192, 1024], P('seq', 'ch')
All inputs are finite; a program needn't handle non-finite values.
Results may differ from a plain program's by a relative error of at most 0.013.
Values may be sent and summed in bfloat16 or wider, within the bound.
No kernel may reach another device: no remote copies, remote signals or barrier semaphores. Data moves between devices by JAX's collectives and lax.ppermute only.
A program may use at most 64 MiB of HBM per device.

v0:
```python
import math
import jax
import jax.numpy as jnp
from jax import lax
from jax.sharding import PartitionSpec as P

epsilon = 1e-05
highest = lax.Precision.HIGHEST


def passed_along(block, axis, distance):
    devices = range(lax.axis_size(axis))
    route = [(i - distance, i) for i in devices if i - distance in devices]
    return lax.ppermute(block, axis, route)


def doubled_gather(block, axis):
    devices = lax.axis_size(axis)
    place = lax.axis_index(axis)
    bits = devices.bit_length() - 1
    assert 1 << bits == devices
    gathered = block
    for bit in reversed(range(bits)):
        route = [(i, i ^ 1 << bit) for i in range(devices)]
        arrived = lax.ppermute(gathered, axis, route)
        lower = place >> bit & 1 == 0
        gathered = jnp.where(lower, jnp.stack([gathered, arrived]), jnp.stack([arrived, gathered]))
    gathered = gathered.transpose(tuple(reversed(range(bits))) + tuple(range(bits, gathered.ndim)))
    return gathered.reshape((devices * block.shape[0],) + block.shape[1:])


def halved_sum(partial, axis):
    devices = lax.axis_size(axis)
    place = lax.axis_index(axis)
    bits = devices.bit_length() - 1
    assert 1 << bits == devices
    rows, width = partial.shape
    share = width // devices
    held = partial.reshape((rows,) + (2,) * bits + (share,))
    held = held.transpose((0,) + tuple(range(bits, 0, -1)) + (bits + 1,)).astype(jnp.float32)
    for bit in range(bits):
        route = [(i, i ^ 1 << bit) for i in range(devices)]
        mine = place >> bit & 1
        kept = lax.dynamic_index_in_dim(held, mine, 1, keepdims=False)
        given = lax.dynamic_index_in_dim(held, 1 - mine, 1, keepdims=False)
        arrived = lax.ppermute(given.astype(jnp.bfloat16), axis, route)
        held = kept + arrived.astype(jnp.float32)
    return held


def to_columns(signals):
    return lax.all_to_all(signals, "seq", split_axis=1, concat_axis=2, tiled=True)


def to_rows(signals):
    count, chans, seq_total = signals.shape
    devices = lax.axis_size("seq")
    local_rows = seq_total // devices
    pieces = signals.reshape(count, chans, devices, local_rows).transpose(2, 0, 1, 3)
    arrived = lax.all_to_all(pieces, "seq", split_axis=0, concat_axis=0, tiled=True)
    return arrived.transpose(1, 3, 0, 2).reshape(count, local_rows, devices * chans)


def turn_table(rows, cols, period, sign):
    turns = jnp.arange(rows, dtype=jnp.int32)[:, None] * jnp.arange(cols, dtype=jnp.int32)[None, :]
    turns = lax.optimization_barrier(turns)
    phases = sign * 2.0 * math.pi / period * (turns % period).astype(jnp.float32)
    return (jnp.cos(phases), jnp.sin(phases))


def fft_sizes(seq_total):
    total = 2 * seq_total
    inner = 1
    while inner * inner < total:
        inner *= 2
    return (total // inner, inner)


def forward_dft(signals):
    count, chans, seq_total = signals.shape
    outer, inner = fft_sizes(seq_total)
    grid = signals.reshape(count, chans, outer // 2, inner)
    cos_out, sin_out = turn_table(outer, outer // 2, outer, 1.0)
    first = jnp.einsum(
        "kn,ucnm->uckm", jnp.concatenate([cos_out, -sin_out], 0), grid, precision=lax.Precision.HIGH
    )
    first_real, first_imag = (first[:, :, :outer], first[:, :, outer:])
    cos_tw, sin_tw = turn_table(outer, inner, outer * inner, 1.0)
    turned_real = first_real * cos_tw + first_imag * sin_tw
    turned_imag = first_imag * cos_tw - first_real * sin_tw
    cos_in, sin_in = turn_table(inner, inner, inner, 1.0)
    rotation = jnp.concatenate(
        [jnp.concatenate([cos_in, -sin_in], 1), jnp.concatenate([sin_in, cos_in], 1)], 0
    )
    joined = jnp.concatenate([turned_real, turned_imag], -1)
    spec = jnp.einsum("uckm,mj->uckj", joined, rotation, precision=lax.Precision.HIGH)
    return (spec[..., :inner], spec[..., inner:])


def inverse_dft(spec_real, spec_imag):
    count, chans, outer, inner = spec_real.shape
    cos_in, sin_in = turn_table(inner, inner, inner, 1.0)
    rotation = jnp.concatenate(
        [jnp.concatenate([cos_in, sin_in], 1), jnp.concatenate([-sin_in, cos_in], 1)], 0
    )
    joined = jnp.concatenate([spec_real, spec_imag], -1)
    back = jnp.einsum("uckj,jm->uckm", joined, rotation, precision=lax.Precision.HIGH)
    back_real, back_imag = (back[..., :inner], back[..., inner:])
    cos_tw, sin_tw = turn_table(outer, inner, outer * inner, 1.0)
    turned_real = back_real * cos_tw - back_imag * sin_tw
    turned_imag = back_imag * cos_tw + back_real * sin_tw
    cos_out, sin_out = turn_table(outer, outer // 2, outer, 1.0)
    grid = jnp.einsum(
        "kn,uckm->ucnm",
        jnp.concatenate([cos_out, -sin_out], 0),
        jnp.concatenate([turned_real, turned_imag], 2),
        precision=lax.Precision.HIGH,
    )
    return grid.reshape(count, chans, outer * inner // 2) / float(outer * inner)


def per_device(
    inputs, norm_gain, in_weight, short_filter, long_filter, conv_bias, out_weight, out_grad
):
    local_rows = inputs.shape[0]
    model_width = inputs.shape[1]
    slab_width = long_filter.shape[1]
    taps = short_filter.shape[1]
    wide_inputs = inputs.astype(jnp.float32)
    inv_rms = lax.rsqrt(jnp.mean(wide_inputs * wide_inputs, axis=1, keepdims=True) + epsilon)
    normed = (wide_inputs * inv_rms * norm_gain).astype(jnp.bfloat16)
    in_panel, out_panel = (
        lax.all_gather(in_weight.reshape(in_weight.shape[0], -1), "seq", axis=0, tiled=True),
        doubled_gather(out_weight.T, "seq").T,
    )
    in_flat = in_panel.reshape(model_width, 3 * slab_width)
    projected = jnp.dot(normed, in_flat, preferred_element_type=jnp.float32)
    projected = projected.astype(jnp.bfloat16).reshape(local_rows, 3, slab_width)
    upper_rim = passed_along(projected[local_rows - (taps - 1) :], "seq", 1)
    extended = jnp.concatenate([upper_rim, projected], 0).astype(jnp.float32)
    mixed = jnp.zeros((local_rows, 3, slab_width), jnp.float32)
    for offset in range(taps):
        begin = taps - 1 - offset
        mixed = mixed + short_filter[:, offset, :][None] * extended[begin : begin + local_rows]
    query_br = mixed[:, 0]
    key_br = mixed[:, 1]
    value_br = mixed[:, 2]
    product = key_br * value_br
    gate_grad = jnp.dot(out_grad, out_panel.T, preferred_element_type=jnp.float32)
    carried = gate_grad * query_br
    filt_real, filt_imag = forward_dft(to_columns(long_filter.T[None]))
    filt_real, filt_imag = (filt_real[0], filt_imag[0])
    columns = to_columns(jnp.stack([product, carried]).transpose(0, 2, 1))
    all_real, all_imag = forward_dft(columns)
    sig_real, grad_real = (all_real[0], all_real[1])
    sig_imag, grad_imag = (all_imag[0], all_imag[1])
    conv_real = sig_real * filt_real - sig_imag * filt_imag
    conv_imag = sig_real * filt_imag + sig_imag * filt_real
    back_real = grad_real * filt_real + grad_imag * filt_imag
    back_imag = grad_imag * filt_real - grad_real * filt_imag
    pair_real = grad_real * sig_real + grad_imag * sig_imag
    pair_imag = grad_imag * sig_real - grad_real * sig_imag
    outs = inverse_dft(
        jnp.stack([conv_real, back_real, pair_real]), jnp.stack([conv_imag, back_imag, pair_imag])
    )
    returned = to_rows(outs)
    conv_out = returned[0]
    back_conv = returned[1]
    filter_grad = returned[2] * float(local_rows * lax.axis_size("seq")) ** (-0.5)
    biased = conv_out + conv_bias * product
    gated = (query_br * biased).astype(jnp.bfloat16)
    partial_out = jnp.dot(gated, out_panel, preferred_element_type=jnp.float32)
    source_grad = back_conv + conv_bias * carried
    mixed_grad = jnp.stack([gate_grad * biased, source_grad * value_br, source_grad * key_br], 1)
    lower_rim = passed_along(mixed_grad[: taps - 1], "seq", -1)
    extended_back = jnp.concatenate([mixed_grad, lower_rim], 0)
    proj_grad = jnp.zeros((local_rows, 3, slab_width), jnp.float32)
    for offset in range(taps):
        proj_grad = (
            proj_grad
            + short_filter[:, offset, :][None] * extended_back[offset : offset + local_rows]
        )
    proj_grad = proj_grad.astype(jnp.bfloat16).reshape(local_rows, 3 * slab_width)
    partial_grad = jnp.dot(proj_grad, in_flat.T, preferred_element_type=jnp.float32)
    ch_size = lax.axis_size("ch")
    feature_share = model_width // ch_size
    partial_inner = jnp.sum(partial_grad * (norm_gain * wide_inputs), axis=1, keepdims=True)
    inner_high = partial_inner.astype(jnp.bfloat16)
    inner_low = (partial_inner - inner_high.astype(jnp.float32)).astype(jnp.bfloat16)
    extra = jnp.concatenate(
        [inner_high, inner_low, jnp.zeros((local_rows, 126), jnp.bfloat16)], axis=1
    )
    payload = jnp.concatenate(
        [
            partial_out.astype(jnp.bfloat16)
            .reshape(local_rows, ch_size, feature_share)
            .transpose(1, 0, 2),
            partial_grad.astype(jnp.bfloat16)
            .reshape(local_rows, ch_size, feature_share)
            .transpose(1, 0, 2),
            jnp.broadcast_to(extra[None], (ch_size, local_rows, 128)),
        ],
        axis=2,
    )
    reduced = lax.psum_scatter(payload, "ch", scatter_dimension=0).astype(jnp.float32)
    summed = reduced[:, :feature_share]
    norm_grad = reduced[:, feature_share : 2 * feature_share]
    inner_at = 2 * feature_share
    inner_term = (
        reduced[:, inner_at : inner_at + 1] + reduced[:, inner_at + 1 : inner_at + 2]
    ) / model_width
    feature_begin = lax.axis_index("ch") * feature_share
    residual = lax.dynamic_slice_in_dim(wide_inputs, feature_begin, feature_share, 1)
    block_out = (residual + summed).astype(jnp.bfloat16)
    gain_share = lax.dynamic_slice_in_dim(norm_gain, feature_begin, feature_share, 0)
    inputs_share = lax.dynamic_slice_in_dim(wide_inputs, feature_begin, feature_share, 1)
    grad_share = lax.dynamic_slice_in_dim(out_grad, feature_begin, feature_share, 1)
    weighted = norm_grad * gain_share
    in_grad_share = (
        grad_share.astype(jnp.float32) + weighted * inv_rms - inputs_share * inv_rms**3 * inner_term
    ).astype(jnp.bfloat16)
    in_grad = (
        doubled_gather(in_grad_share[None], "ch")
        .transpose(1, 0, 2)
        .reshape(local_rows, model_width)
    )
    return (block_out, in_grad, filter_grad)


def solution(mesh):
    return jax.shard_map(
        per_device,
        mesh=mesh,
        in_specs=(
            P("seq", None),
            P(),
            P("seq", None, "ch"),
            P(None, None, "ch"),
            P("seq", "ch"),
            P("ch"),
            P("ch", "seq"),
            P("seq", None),
        ),
        out_specs=(P("seq", "ch"), P("seq", None), P("seq", "ch")),
        check_vma=False,
    )
```

profile of v0, /device:TPU:2, one launch (start us, length us, event | category | flops | bytes accessed | tf_op | source)
XLA Modules:
  0.0 249.4 jit_solution(18105231908628929155)
XLA Ops:
  7.2 1.5 copy.156
  8.8 2.2 collective-permute-start.1
  11.0 1.7 copy.126
  12.6 11.2 %all-to-all-start.1 = ((f32[1,256,128]{2,0,1:T(1,128)}), f32[1,256,128]{2,0,1:T(1,128)}, u32[]{:S(2)}, u32[]{:S(2)}) async-start(f32[1,256,128]{2,0,1:T(1,128)} %bitcast.1), calls=%async_computation.1 | async-start | bytes 262144 | tf_op jit(solution)/shard_map/all_to_all | solution.py:52
  28.5 2.5 %collective-permute-done.2 = bf16[2,64,256]{2,1,0:T(8,128)(2,1)S(1)} collective-permute-done((bf16[2,64,256]{2,1,0:T(8,128)(2,1)S(1)}, bf16[2,64,256]{2,1,0:T(8,128)(2,1)S(1)}, u32[]{:S(2)}, u32[]{:S(2)}) %collective-permute-start.2) | collective-permute-done | bytes 65568 | tf_op jit(solution)/shard_map/ppermute | solution.py:25
  31.0 5.2 %collective-permute-start.3 = (bf16[2,2,64,256]{3,2,0,1:T(8,128)(2,1)S(1)}, bf16[2,2,64,256]{3,2,0,1:T(8,128)(2,1)S(1)}, u32[]{:S(2)}, u32[]{:S(2)}) collective-permute-start(bf16[2,2,64,256]{3,2,0,1:T(8,128)(2,1)S(1)} %maximum_select_fusion.7), channel_id=1, source_target_pairs={{0,32},{4,36},{8,40},{12,44},{16,48},{20,52},{24,56},{28,60},{32,0... | collective-permute-start | bytes 393224 | tf_op jit(solution)/shard_map/ppermute | solution.py:25
  36.3 6.4 %collective-permute-done.3 = bf16[2,2,64,256]{3,2,0,1:T(8,128)(2,1)S(1)} collective-permute-done((bf16[2,2,64,256]{3,2,0,1:T(8,128)(2,1)S(1)}, bf16[2,2,64,256]{3,2,0,1:T(8,128)(2,1)S(1)}, u32[]{:S(2)}, u32[]{:S(2)}) %collective-permute-start.3) | collective-permute-done | bytes 131104 | tf_op jit(solution)/shard_map/ppermute | solution.py:25
  42.7 3.4 %collective-permute-start.4 = (bf16[2,2,2,64,256]{4,3,0,1,2:T(8,128)(2,1)S(1)}, bf16[2,2,2,64,256]{4,3,0,1,2:T(8,128)(2,1)S(1)}, u32[]{:S(2)}, u32[]{:S(2)}) collective-permute-start(bf16[2,2,2,64,256]{4,3,0,1,2:T(8,128)(2,1)S(1)} %maximum_select_fusion.6), channel_id=1, source_target_pairs={{0,16},{4,20},{8,24},{12,28},{16,0},{20,4},{24,8},{28,12},{32,48},... | collective-permute-start | bytes 786440 | tf_op jit(solution)/shard_map/ppermute | solution.py:25
  46.3 11.2 %collective-permute-done.4 = bf16[2,2,2,64,256]{4,3,0,1,2:T(8,128)(2,1)S(1)} collective-permute-done((bf16[2,2,2,64,256]{4,3,0,1,2:T(8,128)(2,1)S(1)}, bf16[2,2,2,64,256]{4,3,0,1,2:T(8,128)(2,1)S(1)}, u32[]{:S(2)}, u32[]{:S(2)}) %collective-permute-start.4) | collective-permute-done | bytes 262176 | tf_op jit(solution)/shard_map/ppermute | solution.py:25
  60.3 11.2 %collective-permute-done.5 = bf16[2,2,2,2,64,256]{5,4,0,1,2,3:T(8,128)(2,1)S(1)} collective-permute-done((bf16[2,2,2,2,64,256]{5,4,0,1,2,3:T(8,128)(2,1)S(1)}, bf16[2,2,2,2,64,256]{5,4,0,1,2,3:T(8,128)(2,1)S(1)}, u32[]{:S(2)}, u32[]{:S(2)}) %collective-permute-start.5) | collective-permute-done | bytes 524320 | tf_op jit(solution)/shard_map/ppermute | solution.py:25
  74.6 25.0 %all-gather.2.cloned.1.call-done = bf16[4096,768]{1,0:T(8,128)(2,1)} async-done(((bf16[64,768]{1,0:T(8,128)(2,1)}), bf16[4096,768]{1,0:T(8,128)(2,1)}) %all-gather.2.cloned.1.call-update) | async-done | bytes 6291472 | tf_op jit(solution)/shard_map/all_gather | solution.py:133
  99.6 3.9 %convolution_convert_fusion.1 = bf16[128,768]{1,0:T(8,128)(2,1)S(1)} fusion(bf16[4096,768]{1,0:T(8,128)(2,1)} %all-gather.2.cloned.1.call-done, bf16[128,4096]{1,0:T(8,128)(2,1)S(1)} %copy-done, f32[4096]{0:T(1024)S(1)} %copy-done.17, f32[128]{0:T(128)S(1)} %get-tuple-element.53), kind=kOutput, calls=%fused_computation.26 | convolution fusion | flops 807501824 | bytes 7553536 | tf_op jit(solution)/shard_map/dot_general | solution.py:137
  104.1 2.1 collective-permute-start
  107.8 3.6 %collective-permute-done = bf16[2,3,256]{2,0,1:T(2,128)(2,1)S(1)} collective-permute-done((bf16[2,3,256]{2,0,1:T(2,128)(2,1)}, bf16[2,3,256]{2,0,1:T(2,128)(2,1)S(1)}, u32[]{:S(2)}, u32[]{:S(2)}) %collective-permute-start) | collective-permute-done | bytes 3104 | tf_op jit(solution)/shard_map/ppermute | solution.py:14
  112.3 1.8 copy.120
  114.1 6.5 %all-to-all-start = ((f32[2,256,128]{2,0,1:T(2,128)}), f32[2,256,128]{2,0,1:T(2,128)}, u32[]{:S(2)}, u32[]{:S(2)}) async-start(f32[2,256,128]{2,0,1:T(2,128)} %copy.120), calls=%async_computation | async-start | bytes 524288 | tf_op jit(solution)/shard_map/all_to_all | solution.py:52
  124.4 2.3 convolution_bitcast_fusion.1
  126.8 5.3 %all-to-all-done = f32[2,256,128]{2,0,1:T(2,128)} async-done(((f32[2,256,128]{2,0,1:T(2,128)}), f32[2,256,128]{2,0,1:T(2,128)}, u32[]{:S(2)}, u32[]{:S(2)}) %all-to-all-start) | async-done | bytes 262176 | tf_op jit(solution)/shard_map/all_to_all | solution.py:52
  132.1 1.6 convolution_bitcast_fusion
  139.3 6.6 %all-to-all-start.2 = ((f32[64,3,4,128]{3,2,1,0:T(4,128)}), f32[64,3,4,128]{3,2,1,0:T(4,128)}, u32[]{:S(2)}, u32[]{:S(2)}) async-start(f32[64,3,4,128]{3,2,1,0:T(4,128)} %copy.131), calls=%async_computation.2 | async-start | bytes 786432 | tf_op jit(solution)/shard_map/all_to_all | solution.py:60
  146.6 13.4 %all-to-all-done.2 = f32[64,3,4,128]{3,2,1,0:T(4,128)} async-done(((f32[64,3,4,128]{3,2,1,0:T(4,128)}), f32[64,3,4,128]{3,2,1,0:T(4,128)}, u32[]{:S(2)}, u32[]{:S(2)}) %all-to-all-start.2) | async-done | bytes 393248 | tf_op jit(solution)/shard_map/all_to_all | solution.py:60
  160.0 1.8 slice_multiply_fusion.6
  161.7 1.7 copy.132
  163.4 1.7 copy.134
  165.1 1.7 copy.135
  167.9 2.9 %collective-permute-start.7 = (f32[2,3,256]{2,0,1:T(2,128)S(1)}, f32[2,3,256]{2,0,1:T(2,128)S(1)}, u32[]{:S(2)}, u32[]{:S(2)}) collective-permute-start(f32[2,3,256]{2,0,1:T(2,128)S(1)} %slice.165), channel_id=1, source_target_pairs={{4,0},{8,4},{12,8},{16,12},{20,16},{24,20},{28,24},{32,28},{36,32}... | collective-permute-start | bytes 18440 | tf_op jit(solution)/shard_map/ppermute | solution.py:14
  172.5 5.0 %fusion.90 = (bf16[128,4096]{1,0:T(8,128)(2,1)S(1)}, f32[128]{0:T(128)S(1)}) fusion(bf16[128,4096]{1,0:T(8,128)(2,1)S(1)} %copy-done, f32[4096]{0:T(1024)S(1)} %copy-done.18, bf16[128,768]{0,1:T(8,128)(2,1)S(1)} %bitcast.206, bf16[4096,768]{1,0:T(8,128)(2,1)} %all-gather.2.cloned.1.call-done), kind=kOutput, calls=%fused_computation.176 | convolution fusion | flops 807927680 | bytes 8602112 | tf_op jit(solution)/shard_map/dot_general | solution.py:184
  180.7 1.6 pad_maximum_fusion
  182.6 32.0 %reduce-scatter.2.cloned.1.call-done = bf16[1,128,2176]{2,1,0:T(8,128)(2,1)} async-done(((bf16[4,128,2176]{2,1,0:T(8,128)(2,1)}), bf16[1,128,2176]{2,1,0:T(8,128)(2,1)}) %reduce-scatter.2.cloned.1.call-update) | async-done | bytes 557072 | tf_op jit(solution)/shard_map/reduce_scatter | solution.py:205
  216.0 1.9 fusion.29
  219.3 8.0 %collective-permute-done.8 = bf16[1,128,1024]{2,1,0:T(8,128)(2,1)S(1)} collective-permute-done((bf16[1,128,1024]{2,1,0:T(8,128)(2,1)S(1)}, bf16[1,128,1024]{2,1,0:T(8,128)(2,1)S(1)}, u32[]{:S(2)}, u32[]{:S(2)}) %collective-permute-start.8) | collective-permute-done | bytes 262176 | tf_op jit(solution)/shard_map/ppermute | solution.py:25
  228.6 11.7 %collective-permute-done.9 = bf16[2,1,128,1024]{3,2,1,0:T(8,128)(2,1)S(1)} collective-permute-done((bf16[2,1,128,1024]{3,2,1,0:T(8,128)(2,1)S(1)}, bf16[2,1,128,1024]{3,2,1,0:T(8,128)(2,1)S(1)}, u32[]{:S(2)}, u32[]{:S(2)}) %collective-permute-start.9) | collective-permute-done | bytes 524320 | tf_op jit(solution)/shard_map/ppermute | solution.py:25
  (137 shorter events, 36.0 us)
Async XLA Ops:
  7.2 92.5 %all-gather.2.cloned.1.call-start = ((), (), s32[]{:S(2)}) async-start(), calls=%async_computation.4 | async-start | bytes 6389760 | tf_op jit(solution)/shard_map/all_gather | solution.py:133
  8.8 16.6 %collective-permute-start.1 = (bf16[64,256]{1,0:T(8,128)(2,1)}, bf16[64,256]{1,0:T(8,128)(2,1)S(1)}, u32[]{:S(2)}, u32[]{:S(2)}) collective-permute-start(bf16[64,256]{1,0:T(8,128)(2,1)} %bitcast.213), channel_id=1, source_target_pairs={{0,128},{4,132},{8,136},{12,140},{16,144},{20,148},{24,152},{28,15... | collective-permute-start | bytes 98312 | tf_op jit(solution)/shard_map/ppermute | solution.py:25
  12.6 101.5 %all-to-all-start.1 = ((f32[1,256,128]{2,0,1:T(1,128)}), f32[1,256,128]{2,0,1:T(1,128)}, u32[]{:S(2)}, u32[]{:S(2)}) async-start(f32[1,256,128]{2,0,1:T(1,128)} %bitcast.1), calls=%async_computation.1 | async-start | bytes 262144 | tf_op jit(solution)/shard_map/all_to_all | solution.py:52
  26.2 4.8 %collective-permute-start.2 = (bf16[2,64,256]{2,1,0:T(8,128)(2,1)S(1)}, bf16[2,64,256]{2,1,0:T(8,128)(2,1)S(1)}, u32[]{:S(2)}, u32[]{:S(2)}) collective-permute-start(bf16[2,64,256]{2,1,0:T(8,128)(2,1)S(1)} %maximum_select_fusion.8), channel_id=1, source_target_pairs={{0,64},{4,68},{8,72},{12,76},{16,80},{20,84},{24,88},{28,92},{32,9... | collective-permute-start | bytes 196616 | tf_op jit(solution)/shard_map/ppermute | solution.py:25
  31.0 11.7 %collective-permute-start.3 = (bf16[2,2,64,256]{3,2,0,1:T(8,128)(2,1)S(1)}, bf16[2,2,64,256]{3,2,0,1:T(8,128)(2,1)S(1)}, u32[]{:S(2)}, u32[]{:S(2)}) collective-permute-start(bf16[2,2,64,256]{3,2,0,1:T(8,128)(2,1)S(1)} %maximum_select_fusion.7), channel_id=1, source_target_pairs={{0,32},{4,36},{8,40},{12,44},{16,48},{20,52},{24,56},{28,60},{32,0... | collective-permute-start | bytes 393224 | tf_op jit(solution)/shard_map/ppermute | solution.py:25
  42.7 14.7 %collective-permute-start.4 = (bf16[2,2,2,64,256]{4,3,0,1,2:T(8,128)(2,1)S(1)}, bf16[2,2,2,64,256]{4,3,0,1,2:T(8,128)(2,1)S(1)}, u32[]{:S(2)}, u32[]{:S(2)}) collective-permute-start(bf16[2,2,2,64,256]{4,3,0,1,2:T(8,128)(2,1)S(1)} %maximum_select_fusion.6), channel_id=1, source_target_pairs={{0,16},{4,20},{8,24},{12,28},{16,0},{20,4},{24,8},{28,12},{32,48},... | collective-permute-start | bytes 786440 | tf_op jit(solution)/shard_map/ppermute | solution.py:25
  57.5 14.0 %collective-permute-start.5 = (bf16[2,2,2,2,64,256]{5,4,0,1,2,3:T(8,128)(2,1)S(1)}, bf16[2,2,2,2,64,256]{5,4,0,1,2,3:T(8,128)(2,1)S(1)}, u32[]{:S(2)}, u32[]{:S(2)}) collective-permute-start(bf16[2,2,2,2,64,256]{5,4,0,1,2,3:T(8,128)(2,1)S(1)} %maximum_select_fusion.3), channel_id=1, source_target_pairs={{0,8},{4,12},{8,0},{12,4},{16,24},{20,28},{24,16},{28,20},{32,40},... | collective-permute-start | bytes 1572872 | tf_op jit(solution)/shard_map/ppermute | solution.py:25
  58.7 1.4 copy-start.7
  58.7 1.4 copy-start.9
  60.3 11.5 %copy-start = (bf16[128,4096]{1,0:T(8,128)(2,1)S(1)}, bf16[128,4096]{1,0:T(8,128)(2,1)}, u32[]{:S(2)}) copy-start(bf16[128,4096]{1,0:T(8,128)(2,1)} %param.8) | copy-start | bytes 3145732
  71.7 2.8 %collective-permute-start.6 = (bf16[2,2,2,2,2,64,256]{6,5,0,1,2,3,4:T(8,128)(2,1)S(1)}, bf16[2,2,2,2,2,64,256]{6,5,0,1,2,3,4:T(8,128)(2,1)S(1)}, u32[]{:S(2)}, u32[]{:S(2)}) collective-permute-start(bf16[2,2,2,2,2,64,256]{6,5,0,1,2,3,4:T(8,128)(2,1)S(1)} %maximum_select_fusion.1), channel_id=1, source_target_pairs={{0,4},{4,0},{8,12},{12,8},{16,20},{20,16},{24,28},{28,24},{32,36},... | collective-permute-start | bytes 3145736 | tf_op jit(solution)/shard_map/ppermute | solution.py:25
  72.6 27.0 %copy-start.22 = (f32[128]{0:T(128)}, f32[128]{0:T(128)S(1)}, u32[]{:S(2)}) copy-start(f32[128]{0:T(128)S(1)} %get-tuple-element.53) | copy-start | bytes 1540
  74.4 25.2 %copy-start.17 = (f32[4096]{0:T(1024)S(1)}, f32[4096]{0:T(1024)}, u32[]{:S(2)}) copy-start(f32[4096]{0:T(1024)} %param.9) | copy-start | bytes 49156
  99.6 6.6 %copy-start.2 = (bf16[128,4096]{1,0:T(8,128)(2,1)S(1)}, bf16[128,4096]{1,0:T(8,128)(2,1)}, u32[]{:S(2)}) copy-start(bf16[128,4096]{1,0:T(8,128)(2,1)} %param.15) | copy-start | bytes 3145732
  104.1 7.2 %collective-permute-start = (bf16[2,3,256]{2,0,1:T(2,128)(2,1)}, bf16[2,3,256]{2,0,1:T(2,128)(2,1)S(1)}, u32[]{:S(2)}, u32[]{:S(2)}) collective-permute-start(bf16[2,3,256]{2,0,1:T(2,128)(2,1)} %bitcast.6), channel_id=1, source_target_pairs={{0,4},{4,8},{8,12},{12,16},{16,20},{20,24},{24,28},{28,32},{32,36}... | collective-permute-start | bytes 9224 | tf_op jit(solution)/shard_map/ppermute | solution.py:14
  107.7 3.8 %copy-start.3 = (f32[128,256]{1,0:T(8,128)S(1)}, f32[128,256]{1,0:T(8,128)}, u32[]{:S(2)}) copy-start(f32[128,256]{1,0:T(8,128)} %convolution_bitcast_fusion.3) | copy-start | bytes 393220
  114.1 17.9 %all-to-all-start = ((f32[2,256,128]{2,0,1:T(2,128)}), f32[2,256,128]{2,0,1:T(2,128)}, u32[]{:S(2)}, u32[]{:S(2)}) async-start(f32[2,256,128]{2,0,1:T(2,128)} %copy.120), calls=%async_computation | async-start | bytes 524288 | tf_op jit(solution)/shard_map/all_to_all | solution.py:52
  132.1 2.7 %copy-start.4 = (f32[128,128]{1,0:T(8,128)S(1)}, f32[128,128]{1,0:T(8,128)}, u32[]{:S(2)}) copy-start(f32[128,128]{1,0:T(8,128)} %get-tuple-element.42) | copy-start | bytes 196612
  132.1 2.7 %copy-start.5 = (f32[128,128]{1,0:T(8,128)S(1)}, f32[128,128]{1,0:T(8,128)}, u32[]{:S(2)}) copy-start(f32[128,128]{1,0:T(8,128)} %get-tuple-element.44) | copy-start | bytes 196612
  132.1 2.7 %copy-start.6 = (f32[128,128]{1,0:T(8,128)S(1)}, f32[128,128]{1,0:T(8,128)}, u32[]{:S(2)}) copy-start(f32[128,128]{1,0:T(8,128)} %get-tuple-element.46) | copy-start | bytes 196612
  134.7 1.1 copy-start.1
  137.6 29.1 %copy-start.19 = (f32[256]{0:T(256)S(1)}, f32[256]{0:T(256)}, u32[]{:S(2)}) copy-start(f32[256]{0:T(256)} %param.13) | copy-start | bytes 3076
  139.3 20.7 %all-to-all-start.2 = ((f32[64,3,4,128]{3,2,1,0:T(4,128)}), f32[64,3,4,128]{3,2,1,0:T(4,128)}, u32[]{:S(2)}, u32[]{:S(2)}) async-start(f32[64,3,4,128]{3,2,1,0:T(4,128)} %copy.131), calls=%async_computation.2 | async-start | bytes 786432 | tf_op jit(solution)/shard_map/all_to_all | solution.py:60
  145.9 68.7 %reduce-scatter.2.cloned.1.call-start = ((), (), s32[]{:S(2)}) async-start(), calls=%async_computation.5 | async-start | bytes 2785280 | tf_op jit(solution)/shard_map/reduce_scatter | solution.py:205
  166.7 4.1 %copy-start.15 = (f32[128,1,256]{2,0,1:T(8,128)S(1)}, f32[128,1,256]{2,0,1:T(8,128)}, u32[]{:S(2)}) copy-start(f32[128,1,256]{2,0,1:T(8,128)} %copy.132) | copy-start | bytes 393220
  167.9 4.2 %collective-permute-start.7 = (f32[2,3,256]{2,0,1:T(2,128)S(1)}, f32[2,3,256]{2,0,1:T(2,128)S(1)}, u32[]{:S(2)}, u32[]{:S(2)}) collective-permute-start(f32[2,3,256]{2,0,1:T(2,128)S(1)} %slice.165), channel_id=1, source_target_pairs={{4,0},{8,4},{12,8},{16,12},{20,16},{24,20},{28,24},{32,28},{36,32}... | collective-permute-start | bytes 18440 | tf_op jit(solution)/shard_map/ppermute | solution.py:14
  177.5 3.1 %copy-start.20 = (bf16[128]{0:T(256)(128)(2,1)S(1)}, bf16[128]{0:T(256)(128)(2,1)}, u32[]{:S(2)}) copy-start(bf16[128]{0:T(256)(128)(2,1)} %pad.17.clone) | copy-start | bytes 772
  182.3 33.6 %copy-start.21 = (f32[128]{0:T(128)S(1)}, f32[128]{0:T(128)}, u32[]{:S(2)}) copy-start(f32[128]{0:T(128)} %get-tuple-element.52) | copy-start | bytes 1540
  182.4 33.6 %copy-start.23 = (f32[128]{0:T(128)S(1)}, f32[128]{0:T(128)}, u32[]{:S(2)}) copy-start(f32[128]{0:T(128)} %copy-done.22) | copy-start | bytes 1540
  215.8 12.0 %copy-start.16 = (f32[1,128,64,4]{1,3,0,2:T(4,128)S(1)}, f32[1,128,64,4]{1,3,0,2:T(4,128)}, u32[]{:S(2)}) copy-start(f32[1,128,64,4]{1,3,0,2:T(4,128)} %get-tuple-element.35) | copy-start | bytes 393220
  217.9 9.5 %collective-permute-start.8 = (bf16[1,128,1024]{2,1,0:T(8,128)(2,1)S(1)}, bf16[1,128,1024]{2,1,0:T(8,128)(2,1)S(1)}, u32[]{:S(2)}, u32[]{:S(2)}) collective-permute-start(bf16[1,128,1024]{2,1,0:T(8,128)(2,1)S(1)} %bitcast.192), channel_id=1, source_target_pairs={{0,2},{1,3},{2,0},{3,1},{4,6},{5,7},{6,4},{7,5},{8,10},{9,11},{10,... | collective-permute-start | bytes 786440 | tf_op jit(solution)/shard_map/ppermute | solution.py:25
  227.5 12.8 %collective-permute-start.9 = (bf16[2,1,128,1024]{3,2,1,0:T(8,128)(2,1)S(1)}, bf16[2,1,128,1024]{3,2,1,0:T(8,128)(2,1)S(1)}, u32[]{:S(2)}, u32[]{:S(2)}) collective-permute-start(bf16[2,1,128,1024]{3,2,1,0:T(8,128)(2,1)S(1)} %maximum_select_fusion.5), channel_id=1, source_target_pairs={{0,1},{1,0},{2,3},{3,2},{4,5},{5,4},{6,7},{7,6},{8,9},{9,8},{10,11... | collective-permute-start | bytes 1572872 | tf_op jit(solution)/shard_map/ppermute | solution.py:25
  (7 other events, 5.3 us)
Sparse Core Ops, SparseCore 0:
  11.3 88.2 all-gather.1
  182.5 32.1 reduce-scatter.1
where the time goes:
time: 251 us; the launch traced here: 249 us
  waiting for transfers between devices  132 us (53%)
  starting transfers between devices  42.9 us (17%)
  local copies, waits for them, and re-layouts  22.1 us (9%)
  other arithmetic  18.8 us (7%)
  matrix products  18.6 us (7%)
  between operations  14.7 us (6%)
    ppermute x8, waiting for transfers between devices, doubled_gather(): arrived = lax.ppermute(gathered, axis, route)  52.5 us
    reduce_scatter x1, waiting for transfers between devices, per_device(): lax.psum_scatter(payload, 'ch', scatter_dimension=0).astype(jnp.float32)  32 us
    all_gather x1, waiting for transfers between devices, per_device(): lax.all_gather(in_weight.reshape(in_weight.shape[0], -1), 'seq', axis=0,...  25 us
    all_to_all x2, starting transfers between devices, to_columns(): lax.all_to_all(signals, 'seq', split_axis=1, concat_axis=2, tiled=True)  17.7 us
    ppermute x8, starting transfers between devices, doubled_gather(): arrived = lax.ppermute(gathered, axis, route)  13.5 us
    all_to_all x1, waiting for transfers between devices, to_rows(): lax.all_to_all(pieces, 'seq', split_axis=0, concat_axis=0, tiled=True)  13.4 us
    all_to_all x1, starting transfers between devices, to_rows(): lax.all_to_all(pieces, 'seq', split_axis=0, concat_axis=0, tiled=True)  6.64 us
    all_to_all x2, waiting for transfers between devices, to_columns(): lax.all_to_all(signals, 'seq', split_axis=1, concat_axis=2, tiled=True)  5.28 us
  transfers between devices with their start and end apart: 15, of which 13 were waited for; matrix products, arithmetic and copies ran while one was open for 11% of the time, Pallas kernels for 0%

commit v1 on v0

--- a/solution.py
+++ b/solution.py
@@ -129,8 +129,18 @@
     wide_inputs = inputs.astype(jnp.float32)
     inv_rms = lax.rsqrt(jnp.mean(wide_inputs * wide_inputs, axis=1, keepdims=True) + epsilon)
     normed = (wide_inputs * inv_rms * norm_gain).astype(jnp.bfloat16)
+
+    def point_record_now(sheet):
+        x_new = lax.all_to_all(
+            jnp.stack([sheet for _ in range(lax.axis_size("seq"))], axis=0),
+            axis_name="seq",
+            split_axis=0,
+            concat_axis=0,
+        )
+        return jnp.concatenate(x_new, axis=0)
+
     in_panel, out_panel = (
-        lax.all_gather(in_weight.reshape(in_weight.shape[0], -1), "seq", axis=0, tiled=True),
+        point_record_now(in_weight.reshape(in_weight.shape[0], -1)),
         doubled_gather(out_weight.T, "seq").T,
     )
     in_flat = in_panel.reshape(model_width, 3 * slab_width)

time: 251 us -> 364 us (1.45)
  waiting for transfers between devices: 132 us -> 235 us
  starting transfers between devices: 42.9 us -> 51.6 us
    ppermute x8, waiting for transfers between devices: 52.5 us -> 181 us  [doubled_gather(): arrived = lax.ppermute(gathered, axis, route)]
    all_gather x1 -> x0, waiting for transfers between devices: 25 us -> none  [per_device(): lax.all_gather(in_weight.reshape(in_weight.shape[0], -1), 'seq', axis=0,...]
    all_to_all x0 -> x1, starting transfers between devices: none -> 12.3 us  [point_record_now(): lax.all_to_all(jnp.stack([sheet for _ in range(lax.axis_size('seq'))], ax...]
    ppermute x8, starting transfers between devices: 13.5 us -> 8.18 us  [doubled_gather(): arrived = lax.ppermute(gathered, axis, route)]
    another operation x0 -> x2, local copies, waits for them, and re-layouts: none -> 4.34 us  [point_record_now(): jnp.stack([sheet for _ in range(lax.axis_size('seq'))], axis=0)]
  transfers between devices with their start and end apart: 15 -> 15, of which waited for: 13 -> 12; matrix products, arithmetic and copies ran while one was open for 11% -> 7% of each run, Pallas kernels for 0% -> 0%
where the time goes in v1:
time: 364 us; the launch traced here: 363 us
  waiting for transfers between devices  235 us (65%)
  starting transfers between devices  51.6 us (14%)
  local copies, waits for them, and re-layouts  24.5 us (7%)
  matrix products  19.6 us (5%)
  other arithmetic  16.9 us (5%)
  between operations  14.8 us (4%)
    ppermute x8, waiting for transfers between devices, doubled_gather(): arrived = lax.ppermute(gathered, axis, route)  181 us
    reduce_scatter x1, waiting for transfers between devices, per_device(): lax.psum_scatter(payload, 'ch', scatter_dimension=0).astype(jnp.float32)  31.8 us
    all_to_all x2, starting transfers between devices, to_columns(): lax.all_to_all(signals, 'seq', split_axis=1, concat_axis=2, tiled=True)  19.6 us
    all_to_all x1, waiting for transfers between devices, to_rows(): lax.all_to_all(pieces, 'seq', split_axis=0, concat_axis=0, tiled=True)  13.3 us
    all_to_all x1, starting transfers between devices, point_record_now(): lax.all_to_all(jnp.stack([sheet for _ in range(lax.axis_size('seq'))], ax...  12.3 us
    ppermute x8, starting transfers between devices, doubled_gather(): arrived = lax.ppermute(gathered, axis, route)  8.18 us
  transfers between devices with their start and end apart: 15, of which 12 were waited for; matrix products, arithmetic and copies ran while one was open for 7% of the time, Pallas kernels for 0%

profile of v1, /device:TPU:2, one launch (start us, length us, event | category | flops | bytes accessed | tf_op | source)
XLA Modules:
  0.0 362.6 jit_solution(17371574400792910458)
XLA Ops:
  8.1 3.4 stack.178
  11.5 12.3 %all-to-all-start = ((bf16[64,64,768]{2,1,0:T(8,128)(2,1)}), bf16[64,64,768]{2,1,0:T(8,128)(2,1)}, u32[]{:S(2)}, u32[]{:S(2)}) async-start(bf16[64,64,768]{2,1,0:T(8,128)(2,1)} %stack.178), calls=%async_computation | async-start | bytes 12582912 | tf_op jit(solution)/shard_map/all_to_all | solution.py:134
  23.9 2.4 collective-permute-start.1
  26.9 14.4 %collective-permute-done.1 = bf16[64,256]{1,0:T(8,128)(2,1)S(1)} collective-permute-done((bf16[64,256]{1,0:T(8,128)(2,1)S(1)}, bf16[64,256]{1,0:T(8,128)(2,1)S(1)}, u32[]{:S(2)}, u32[]{:S(2)}) %collective-permute-start.1) | collective-permute-done | bytes 32800 | tf_op jit(solution)/shard_map/ppermute | solution.py:25
  41.9 4.3 %collective-permute-done.2 = bf16[2,64,256]{2,1,0:T(8,128)(2,1)S(1)} collective-permute-done((bf16[2,64,256]{2,1,0:T(8,128)(2,1)S(1)}, bf16[2,64,256]{2,1,0:T(8,128)(2,1)S(1)}, u32[]{:S(2)}, u32[]{:S(2)}) %collective-permute-start.2) | collective-permute-done | bytes 65568 | tf_op jit(solution)/shard_map/ppermute | solution.py:25
  46.2 2.6 collective-permute-start.3
  48.8 121.6 %collective-permute-done.3 = bf16[2,2,64,256]{3,2,0,1:T(8,128)(2,1)S(1)} collective-permute-done((bf16[2,2,64,256]{3,2,0,1:T(8,128)(2,1)S(1)}, bf16[2,2,64,256]{3,2,0,1:T(8,128)(2,1)S(1)}, u32[]{:S(2)}, u32[]{:S(2)}) %collective-permute-start.3) | collective-permute-done | bytes 131104 | tf_op jit(solution)/shard_map/ppermute | solution.py:25
  171.3 11.5 %collective-permute-done.4 = bf16[2,2,2,64,256]{4,3,0,1,2:T(8,128)(2,1)S(1)} collective-permute-done((bf16[2,2,2,64,256]{4,3,0,1,2:T(8,128)(2,1)S(1)}, bf16[2,2,2,64,256]{4,3,0,1,2:T(8,128)(2,1)S(1)}, u32[]{:S(2)}, u32[]{:S(2)}) %collective-permute-start.4) | collective-permute-done | bytes 262176 | tf_op jit(solution)/shard_map/ppermute | solution.py:25
  186.4 8.1 %collective-permute-done.5 = bf16[2,2,2,2,64,256]{5,4,0,1,2,3:T(8,128)(2,1)S(1)} collective-permute-done((bf16[2,2,2,2,64,256]{5,4,0,1,2,3:T(8,128)(2,1)S(1)}, bf16[2,2,2,2,64,256]{5,4,0,1,2,3:T(8,128)(2,1)S(1)}, u32[]{:S(2)}, u32[]{:S(2)}) %collective-permute-start.5) | collective-permute-done | bytes 524320 | tf_op jit(solution)/shard_map/ppermute | solution.py:25
  197.5 9.9 %all-to-all-start.2 = ((f32[1,256,128]{2,0,1:T(1,128)}), f32[1,256,128]{2,0,1:T(1,128)}, u32[]{:S(2)}, u32[]{:S(2)}) async-start(f32[1,256,128]{2,0,1:T(1,128)} %bitcast.1), calls=%async_computation.2 | async-start | bytes 262144 | tf_op jit(solution)/shard_map/all_to_all | solution.py:52
  207.5 3.9 %convolution_convert_fusion.1 = bf16[128,768]{1,0:T(8,128)(2,1)S(1)} fusion(bf16[4096,768]{1,0:T(8,128)(2,1)} %bitcast.6, bf16[128,4096]{1,0:T(8,128)(2,1)S(1)} %copy-done, f32[4096]{0:T(1024)S(1)} %copy-done.24, f32[128]{0:T(128)S(1)} %get-tuple-element.53), kind=kOutput, calls=%fused_computation.26 | convolution fusion | flops 807501824 | bytes 7553536 | tf_op jit(solution)/shard_map/dot_general | solution.py:147
  212.0 2.0 collective-permute-start
  215.5 3.7 %collective-permute-done = bf16[2,3,256]{2,0,1:T(2,128)(2,1)S(1)} collective-permute-done((bf16[2,3,256]{2,0,1:T(2,128)(2,1)}, bf16[2,3,256]{2,0,1:T(2,128)(2,1)S(1)}, u32[]{:S(2)}, u32[]{:S(2)}) %collective-permute-start) | collective-permute-done | bytes 3104 | tf_op jit(solution)/shard_map/ppermute | solution.py:14
  220.2 1.8 copy.120
  221.9 9.6 %all-to-all-start.1 = ((f32[2,256,128]{2,0,1:T(2,128)}), f32[2,256,128]{2,0,1:T(2,128)}, u32[]{:S(2)}, u32[]{:S(2)}) async-start(f32[2,256,128]{2,0,1:T(2,128)} %copy.120), calls=%async_computation.1 | async-start | bytes 524288 | tf_op jit(solution)/shard_map/all_to_all | solution.py:52
  235.4 2.3 convolution_bitcast_fusion.1
  237.7 5.3 %all-to-all-done.1 = f32[2,256,128]{2,0,1:T(2,128)} async-done(((f32[2,256,128]{2,0,1:T(2,128)}), f32[2,256,128]{2,0,1:T(2,128)}, u32[]{:S(2)}, u32[]{:S(2)}) %all-to-all-start.1) | async-done | bytes 262176 | tf_op jit(solution)/shard_map/all_to_all | solution.py:52
  243.0 1.6 convolution_bitcast_fusion
  250.2 6.6 %all-to-all-start.3 = ((f32[64,3,4,128]{3,2,1,0:T(4,128)}), f32[64,3,4,128]{3,2,1,0:T(4,128)}, u32[]{:S(2)}, u32[]{:S(2)}) async-start(f32[64,3,4,128]{3,2,1,0:T(4,128)} %copy.131), calls=%async_computation.3 | async-start | bytes 786432 | tf_op jit(solution)/shard_map/all_to_all | solution.py:60
  257.6 13.3 %all-to-all-done.3 = f32[64,3,4,128]{3,2,1,0:T(4,128)} async-done(((f32[64,3,4,128]{3,2,1,0:T(4,128)}), f32[64,3,4,128]{3,2,1,0:T(4,128)}, u32[]{:S(2)}, u32[]{:S(2)}) %all-to-all-start.3) | async-done | bytes 393248 | tf_op jit(solution)/shard_map/all_to_all | solution.py:60
  270.9 1.8 slice_multiply_fusion.6
  272.7 1.7 copy.135
  274.4 1.7 copy.134
  278.5 2.8 collective-permute-start.7
  281.3 1.7 copy.132
  283.0 1.8 convolution_convert_fusion
  286.0 5.0 %fusion.90 = (bf16[128,4096]{1,0:T(8,128)(2,1)S(1)}, f32[128]{0:T(128)S(1)}) fusion(bf16[128,4096]{1,0:T(8,128)(2,1)S(1)} %copy-done, f32[4096]{0:T(1024)S(1)} %copy-done.25, bf16[128,768]{0,1:T(8,128)(2,1)S(1)} %bitcast.207, bf16[4096,768]{1,0:T(8,128)(2,1)} %bitcast.6), kind=kOutput, calls=%fused_computation.176 | convolution fusion | flops 807927680 | bytes 8602112 | tf_op jit(solution)/shard_map/dot_general | solution.py:194
  294.2 1.6 pad_maximum_fusion
  296.1 31.8 %reduce-scatter.2.cloned.1.call-done = bf16[1,128,2176]{2,1,0:T(8,128)(2,1)} async-done(((bf16[4,128,2176]{2,1,0:T(8,128)(2,1)}), bf16[1,128,2176]{2,1,0:T(8,128)(2,1)}) %reduce-scatter.2.cloned.1.call-update) | async-done | bytes 557072 | tf_op jit(solution)/shard_map/reduce_scatter | solution.py:215
  329.2 1.9 fusion.29
  332.6 8.0 %collective-permute-done.8 = bf16[1,128,1024]{2,1,0:T(8,128)(2,1)S(1)} collective-permute-done((bf16[1,128,1024]{2,1,0:T(8,128)(2,1)S(1)}, bf16[1,128,1024]{2,1,0:T(8,128)(2,1)S(1)}, u32[]{:S(2)}, u32[]{:S(2)}) %collective-permute-start.8) | collective-permute-done | bytes 262176 | tf_op jit(solution)/shard_map/ppermute | solution.py:25
  341.8 11.7 %collective-permute-done.9 = bf16[2,1,128,1024]{3,2,1,0:T(8,128)(2,1)S(1)} collective-permute-done((bf16[2,1,128,1024]{3,2,1,0:T(8,128)(2,1)S(1)}, bf16[2,1,128,1024]{3,2,1,0:T(8,128)(2,1)S(1)}, u32[]{:S(2)}, u32[]{:S(2)}) %collective-permute-start.9) | collective-permute-done | bytes 524320 | tf_op jit(solution)/shard_map/ppermute | solution.py:25
  (153 shorter events, 35.7 us)
Async XLA Ops:
  11.5 12.3 %copy-start.22 = (bf16[256,64]{0,1:T(8,128)(2,1)S(1)}, bf16[256,64]{0,1:T(8,128)(2,1)}, u32[]{:S(2)}) copy-start(bf16[256,64]{0,1:T(8,128)(2,1)} %param.14) | copy-start | bytes 98308
  11.5 14.7 %copy-start.26 = (f32[3,3,256]{2,1,0:T(4,128)S(1)}, f32[3,3,256]{2,1,0:T(4,128)}, u32[]{:S(2)}) copy-start(f32[3,3,256]{2,1,0:T(4,128)} %param.11) | copy-start | bytes 27652
  11.5 186.0 %all-to-all-start = ((bf16[64,64,768]{2,1,0:T(8,128)(2,1)}), bf16[64,64,768]{2,1,0:T(8,128)(2,1)}, u32[]{:S(2)}, u32[]{:S(2)}) async-start(bf16[64,64,768]{2,1,0:T(8,128)(2,1)} %stack.178), calls=%async_computation | async-start | bytes 12582912 | tf_op jit(solution)/shard_map/all_to_all | solution.py:134
  23.9 17.4 %collective-permute-start.1 = (bf16[64,256]{1,0:T(8,128)(2,1)S(1)}, bf16[64,256]{1,0:T(8,128)(2,1)S(1)}, u32[]{:S(2)}, u32[]{:S(2)}) collective-permute-start(bf16[64,256]{1,0:T(8,128)(2,1)S(1)} %bitcast.214), channel_id=1, source_target_pairs={{0,128},{4,132},{8,136},{12,140},{16,144},{20,148},{24,152},{28,15... | collective-permute-start | bytes 98312 | tf_op jit(solution)/shard_map/ppermute | solution.py:25
  41.3 4.9 %collective-permute-start.2 = (bf16[2,64,256]{2,1,0:T(8,128)(2,1)S(1)}, bf16[2,64,256]{2,1,0:T(8,128)(2,1)S(1)}, u32[]{:S(2)}, u32[]{:S(2)}) collective-permute-start(bf16[2,64,256]{2,1,0:T(8,128)(2,1)S(1)} %maximum_select_fusion.8), channel_id=1, source_target_pairs={{0,64},{4,68},{8,72},{12,76},{16,80},{20,84},{24,88},{28,92},{32,9... | collective-permute-start | bytes 196616 | tf_op jit(solution)/shard_map/ppermute | solution.py:25
  46.2 124.2 %collective-permute-start.3 = (bf16[2,2,64,256]{3,2,0,1:T(8,128)(2,1)S(1)}, bf16[2,2,64,256]{3,2,0,1:T(8,128)(2,1)S(1)}, u32[]{:S(2)}, u32[]{:S(2)}) collective-permute-start(bf16[2,2,64,256]{3,2,0,1:T(8,128)(2,1)S(1)} %maximum_select_fusion.7), channel_id=1, source_target_pairs={{0,32},{4,36},{8,40},{12,44},{16,48},{20,52},{24,56},{28,60},{32,0... | collective-permute-start | bytes 393224 | tf_op jit(solution)/shard_map/ppermute | solution.py:25
  48.7 136.7 %copy-start.23 = (f32[128,256]{1,0:T(8,128)S(1)}, f32[128,256]{1,0:T(8,128)}, u32[]{:S(2)}) copy-start(f32[128,256]{1,0:T(8,128)} %param.12) | copy-start | bytes 393220
  170.4 12.3 %collective-permute-start.4 = (bf16[2,2,2,64,256]{4,3,0,1,2:T(8,128)(2,1)S(1)}, bf16[2,2,2,64,256]{4,3,0,1,2:T(8,128)(2,1)S(1)}, u32[]{:S(2)}, u32[]{:S(2)}) collective-permute-start(bf16[2,2,2,64,256]{4,3,0,1,2:T(8,128)(2,1)S(1)} %maximum_select_fusion.6), channel_id=1, source_target_pairs={{0,16},{4,20},{8,24},{12,28},{16,0},{20,4},{24,8},{28,12},{32,48},... | collective-permute-start | bytes 786440 | tf_op jit(solution)/shard_map/ppermute | solution.py:25
  182.8 11.6 %collective-permute-start.5 = (bf16[2,2,2,2,64,256]{5,4,0,1,2,3:T(8,128)(2,1)S(1)}, bf16[2,2,2,2,64,256]{5,4,0,1,2,3:T(8,128)(2,1)S(1)}, u32[]{:S(2)}, u32[]{:S(2)}) collective-permute-start(bf16[2,2,2,2,64,256]{5,4,0,1,2,3:T(8,128)(2,1)S(1)} %maximum_select_fusion.3), channel_id=1, source_target_pairs={{0,8},{4,12},{8,0},{12,4},{16,24},{20,28},{24,16},{28,20},{32,40},... | collective-permute-start | bytes 1572872 | tf_op jit(solution)/shard_map/ppermute | solution.py:25
  184.0 2.2 copy-start.15
  186.3 8.4 %copy-start = (bf16[128,4096]{1,0:T(8,128)(2,1)S(1)}, bf16[128,4096]{1,0:T(8,128)(2,1)}, u32[]{:S(2)}) copy-start(bf16[128,4096]{1,0:T(8,128)(2,1)} %param.8) | copy-start | bytes 3145732
  194.5 2.7 collective-permute-start.6
  195.5 12.0 %copy-start.30 = (f32[128]{0:T(128)}, f32[128]{0:T(128)S(1)}, u32[]{:S(2)}) copy-start(f32[128]{0:T(128)S(1)} %get-tuple-element.53) | copy-start | bytes 1540
  197.3 10.2 %copy-start.24 = (f32[4096]{0:T(1024)S(1)}, f32[4096]{0:T(1024)}, u32[]{:S(2)}) copy-start(f32[4096]{0:T(1024)} %param.9) | copy-start | bytes 49156
  197.5 24.4 %all-to-all-start.2 = ((f32[1,256,128]{2,0,1:T(1,128)}), f32[1,256,128]{2,0,1:T(1,128)}, u32[]{:S(2)}, u32[]{:S(2)}) async-start(f32[1,256,128]{2,0,1:T(1,128)} %bitcast.1), calls=%async_computation.2 | async-start | bytes 262144 | tf_op jit(solution)/shard_map/all_to_all | solution.py:52
  207.5 6.5 %copy-start.8 = (bf16[128,4096]{1,0:T(8,128)(2,1)S(1)}, bf16[128,4096]{1,0:T(8,128)(2,1)}, u32[]{:S(2)}) copy-start(bf16[128,4096]{1,0:T(8,128)(2,1)} %param.15) | copy-start | bytes 3145732
  212.0 7.2 %collective-permute-start = (bf16[2,3,256]{2,0,1:T(2,128)(2,1)}, bf16[2,3,256]{2,0,1:T(2,128)(2,1)S(1)}, u32[]{:S(2)}, u32[]{:S(2)}) collective-permute-start(bf16[2,3,256]{2,0,1:T(2,128)(2,1)} %bitcast.7), channel_id=1, source_target_pairs={{0,4},{4,8},{8,12},{12,16},{16,20},{20,24},{24,28},{28,32},{32,36}... | collective-permute-start | bytes 9224 | tf_op jit(solution)/shard_map/ppermute | solution.py:14
  215.5 3.9 %copy-start.9 = (f32[128,256]{1,0:T(8,128)S(1)}, f32[128,256]{1,0:T(8,128)}, u32[]{:S(2)}) copy-start(f32[128,256]{1,0:T(8,128)} %convolution_bitcast_fusion.3) | copy-start | bytes 393220
  221.9 21.1 %all-to-all-start.1 = ((f32[2,256,128]{2,0,1:T(2,128)}), f32[2,256,128]{2,0,1:T(2,128)}, u32[]{:S(2)}, u32[]{:S(2)}) async-start(f32[2,256,128]{2,0,1:T(2,128)} %copy.120), calls=%async_computation.1 | async-start | bytes 524288 | tf_op jit(solution)/shard_map/all_to_all | solution.py:52
  243.0 2.7 copy-start.10
  243.0 2.7 copy-start.11
  243.0 2.7 copy-start.12
  248.6 27.4 %copy-start.27 = (f32[256]{0:T(256)S(1)}, f32[256]{0:T(256)}, u32[]{:S(2)}) copy-start(f32[256]{0:T(256)} %param.13) | copy-start | bytes 3076
  250.2 20.7 %all-to-all-start.3 = ((f32[64,3,4,128]{3,2,1,0:T(4,128)}), f32[64,3,4,128]{3,2,1,0:T(4,128)}, u32[]{:S(2)}, u32[]{:S(2)}) async-start(f32[64,3,4,128]{3,2,1,0:T(4,128)} %copy.131), calls=%async_computation.3 | async-start | bytes 786432 | tf_op jit(solution)/shard_map/all_to_all | solution.py:60
  256.9 71.0 %reduce-scatter.2.cloned.1.call-start = ((), (), s32[]{:S(2)}) async-start(), calls=%async_computation.5 | async-start | bytes 2785280 | tf_op jit(solution)/shard_map/reduce_scatter | solution.py:215
  278.5 6.4 %collective-permute-start.7 = (f32[2,3,256]{2,0,1:T(2,128)}, f32[2,3,256]{2,0,1:T(2,128)}, u32[]{:S(2)}, u32[]{:S(2)}) collective-permute-start(f32[2,3,256]{2,0,1:T(2,128)} %slice.165), channel_id=1, source_target_pairs={{4,0},{8,4},{12,8},{16,12},{20,16},{24,20},{28,24},{32,28},{36,32}... | collective-permute-start | bytes 18440 | tf_op jit(solution)/shard_map/ppermute | solution.py:14
  291.3 2.8 copy-start.28
  295.8 33.4 %copy-start.29 = (f32[128]{0:T(128)S(1)}, f32[128]{0:T(128)}, u32[]{:S(2)}) copy-start(f32[128]{0:T(128)} %get-tuple-element.52) | copy-start | bytes 1540
  295.8 33.4 %copy-start.31 = (f32[128]{0:T(128)S(1)}, f32[128]{0:T(128)}, u32[]{:S(2)}) copy-start(f32[128]{0:T(128)} %copy-done.30) | copy-start | bytes 1540
  329.0 12.0 %copy-start.21 = (f32[1,128,64,4]{1,3,0,2:T(4,128)S(1)}, f32[1,128,64,4]{1,3,0,2:T(4,128)}, u32[]{:S(2)}) copy-start(f32[1,128,64,4]{1,3,0,2:T(4,128)} %get-tuple-element.35) | copy-start | bytes 393220
  331.1 9.5 %collective-permute-start.8 = (bf16[1,128,1024]{2,1,0:T(8,128)(2,1)S(1)}, bf16[1,128,1024]{2,1,0:T(8,128)(2,1)S(1)}, u32[]{:S(2)}, u32[]{:S(2)}) collective-permute-start(bf16[1,128,1024]{2,1,0:T(8,128)(2,1)S(1)} %bitcast.193), channel_id=1, source_target_pairs={{0,2},{1,3},{2,0},{3,1},{4,6},{5,7},{6,4},{7,5},{8,10},{9,11},{10,... | collective-permute-start | bytes 786440 | tf_op jit(solution)/shard_map/ppermute | solution.py:25
  340.7 12.8 %collective-permute-start.9 = (bf16[2,1,128,1024]{3,2,1,0:T(8,128)(2,1)S(1)}, bf16[2,1,128,1024]{3,2,1,0:T(8,128)(2,1)S(1)}, u32[]{:S(2)}, u32[]{:S(2)}) collective-permute-start(bf16[2,1,128,1024]{3,2,1,0:T(8,128)(2,1)S(1)} %maximum_select_fusion.5), channel_id=1, source_target_pairs={{0,1},{1,0},{2,3},{3,2},{4,5},{5,4},{6,7},{7,6},{8,9},{9,8},{10,11... | collective-permute-start | bytes 1572872 | tf_op jit(solution)/shard_map/ppermute | solution.py:25
  (15 other events, 17.5 us)
Sparse Core Ops, SparseCore 0:
  295.9 31.8 reduce-scatter.1
